TPU v7x, 512 devices: a whole 4x8x8 slice. The times are simulated.
512 devices in a mesh: seq: 64 (over x, z_lo, y), tp: 8 (over z_hi, core).
Axes of the slice: x: 4, y: 8, z: 8 (z_hi: 4, z_lo: 2; z = z_hi * 2 + z_lo), core: 2. Of those that a mesh axis runs over, the one named last changes fastest.
Arguments:
- tokens: bfloat16 [16384, 2048], P('seq', 'tp'), may hold values from -6 to 6
- key_weight: bfloat16 [2048, 2048], P(None, 'tp'), may hold values from -0.125 to 0.125
- value_weight: bfloat16 [2048, 2048], P(None, 'tp'), may hold values from -0.125 to 0.125
- queries: bfloat16 [16384, 2, 2048], P('seq', None, 'tp'), may hold values from -256 to 256
- prompt_pages: int32 [16], replicated, may hold values from 1 to 97, 1024 in all
- page_table: int32 [1024], P('seq'), may hold values from 0 to 1023, as said below
Outputs:
- attended: bfloat16 [16384, 2, 2048], P('seq', None, 'tp')
- cache: bfloat16 [1024, 16, 2, 2048], P('seq', None, None, 'tp')
Inputs may be any that keep to these rules, and one draw needn't show every extreme that they name: `prompt_pages`: lengths of the prompts in pages; they sum to 1024 and the longest has exactly 97 pages. `page_table`: A permutation of the cache pages. Page c is held by owner c // 16 of seq. At most 1 pages of one stream block go to one owner, some block sends exactly 1 to one owner, and every owner receives 256/16 pages.
All inputs are finite; a program needn't handle non-finite values.
Results may differ from a plain program's by a relative error of at most 0.03.
Values may be sent and summed in bfloat16 or wider, within the bound.
No kernel may reach another device: no remote copies, remote signals or barrier semaphores. Data moves between devices by JAX's collectives and lax.ppermute only.
A program may use at most 64 MiB of HBM per device.

v0:
```python
import functools
import math

import jax
import jax.numpy as jnp
from jax import lax
from jax.experimental import pallas as pl
from jax.experimental.pallas import tpu as pltpu
from jax.sharding import PartitionSpec as P


HD = 128
TOPK = 2
PAGE = 16
BACK = 6


def from_behind(value, axis, by):
    peers = lax.axis_size(axis)
    pairs = [(i, i + by) for i in range(peers) if 0 <= i + by < peers]
    return lax.ppermute(value, axis, pairs)


def segment_info(positions, prompt_pages):
    ends = PAGE * jnp.cumsum(prompt_pages)
    below = ends[None, :] <= positions[:, None]
    segment = jnp.sum(below.astype(jnp.int32), axis=1)
    start = jnp.max(jnp.where(below, ends[None, :], 0), axis=1)
    return (segment, positions - start)


def project_kernel(piece_ref, key_weight_ref, value_weight_ref, cosine_ref, sine_ref, out_ref):
    rows = out_ref.shape[0]
    width = key_weight_ref.shape[1]
    share = piece_ref.shape[1]
    keys = jnp.zeros((rows, width), jnp.float32)
    values = jnp.zeros((rows, width), jnp.float32)
    for part in range(piece_ref.shape[0] // rows):
        chunk = piece_ref[part * rows : (part + 1) * rows, :]
        keys = keys + jnp.dot(
            chunk, key_weight_ref[part * share : (part + 1) * share, :],
            preferred_element_type=jnp.float32,
        )
        values = values + jnp.dot(
            chunk, value_weight_ref[part * share : (part + 1) * share, :],
            preferred_element_type=jnp.float32,
        )
    cosine = cosine_ref[...]
    sine = sine_ref[...]
    for head in range(width // HD):
        raw = keys[:, head * HD : (head + 1) * HD]
        turned = raw * cosine + pltpu.roll(raw, HD // 2, 1) * sine
        out_ref[:, head * HD : (head + 1) * HD] = turned.astype(out_ref.dtype)
    out_ref[:, width:] = values.astype(out_ref.dtype)


def project(piece, key_weight, value_weight, offsets):
    rows = offsets.shape[0]
    width = key_weight.shape[1]
    half = HD // 2
    inverse = 10000.0 ** (-(2.0 * jnp.arange(half, dtype=jnp.float32)) / HD)
    angle = offsets.astype(jnp.float32)[:, None] * inverse[None, :]
    cosine = jnp.cos(angle)
    sine = jnp.sin(angle)
    cosine = jnp.concatenate([cosine, cosine], axis=1)
    sine = jnp.concatenate([-sine, sine], axis=1)
    cost = pl.CostEstimate(
        flops=2 * 2 * rows * key_weight.shape[0] * width,
        transcendentals=0,
        bytes_accessed=piece.size * 2 + 2 * key_weight.size * 2 + rows * 2 * width * 2,
    )
    return pl.pallas_call(
        project_kernel,
        out_shape=jax.ShapeDtypeStruct((rows, 2 * width), jnp.bfloat16),
        cost_estimate=cost,
        name="project_rotate",
    )(piece, key_weight, value_weight, cosine, sine)


def masked_scores(query, query_segment, key_segment_ref, key_ref, slot, diagonal, scale):
    rows = query.shape[0]
    product = lax.dot_general(
        query, key_ref[...], (((1,), (1,)), ((), ())), preferred_element_type=jnp.float32
    )
    allowed = query_segment == key_segment_ref[pl.ds(slot, 1), :]
    if diagonal:
        row = lax.broadcasted_iota(jnp.int32, (rows, rows), 0)
        col = lax.broadcasted_iota(jnp.int32, (rows, rows), 1)
        allowed = allowed & (col <= row)
    return jnp.where(allowed, product * scale, -jnp.inf)


def accumulate(scores, value_refs, peak, total, summed):
    for slot, value_ref in enumerate(value_refs):
        weight = jnp.exp(scores(slot) - peak)
        total = total + jnp.sum(weight, axis=1, keepdims=True)
        summed = summed + jnp.dot(
            weight.astype(jnp.bfloat16), value_ref[...], preferred_element_type=jnp.float32
        )
    return total, summed


def first_kernel(query_segment_ref, key_segment_ref, query_ref, *refs, blocks, scale):
    key_refs = refs[:blocks]
    value_refs = refs[blocks : 2 * blocks]
    stats_ref, summed_ref = refs[2 * blocks :]
    query = query_ref[...]
    query_segment = query_segment_ref[...]

    def scores(slot):
        return masked_scores(
            query, query_segment, key_segment_ref, key_refs[slot], slot, slot == 0, scale
        )

    peak = jnp.max(scores(0), axis=1, keepdims=True)
    for slot in range(1, blocks):
        peak = jnp.maximum(peak, jnp.max(scores(slot), axis=1, keepdims=True))
    total = jnp.zeros(peak.shape, jnp.float32)
    summed = jnp.zeros(summed_ref.shape, jnp.float32)
    total, summed = accumulate(scores, value_refs, peak, total, summed)
    combos = stats_ref.shape[1] // 2
    combo = pl.program_id(1) * pl.num_programs(0) + pl.program_id(0)
    lane = lax.broadcasted_iota(jnp.int32, stats_ref.shape, 1)

    @pl.when(combo == 0)
    def _():
        stats_ref[...] = jnp.zeros(stats_ref.shape, jnp.float32)

    stats = jnp.where(lane == combo, peak, stats_ref[...])
    stats_ref[...] = jnp.where(lane == combo + combos, total, stats)
    summed_ref[...] = summed


def second_kernel(
    query_segment_ref, key_segment_ref, query_ref, stats_ref, summed_ref, source_ref, out_ref,
    *, blocks, scale, local_heads,
):
    query_segment = query_segment_ref[...]
    stats = stats_ref[...]
    lane = lax.broadcasted_iota(jnp.int32, stats.shape, 1)
    combos = stats.shape[1] // 2
    span = 2 * local_heads * HD
    for expert in range(TOPK):
        for head in range(local_heads):
            combo = expert * local_heads + head
            columns = slice(combo * HD, (combo + 1) * HD)
            query = query_ref[:, columns]

            def scores(slot):
                key = source_ref[:, slot * span + head * HD : slot * span + (head + 1) * HD]
                product = lax.dot_general(
                    query, key, (((1,), (1,)), ((), ())), preferred_element_type=jnp.float32
                )
                allowed = query_segment == key_segment_ref[pl.ds(slot, 1), :]
                return jnp.where(allowed, product * scale, -jnp.inf)

            first_peak = jnp.sum(jnp.where(lane == combo, stats, 0.0), axis=1, keepdims=True)
            first_total = jnp.sum(
                jnp.where(lane == combo + combos, stats, 0.0), axis=1, keepdims=True
            )
            peak = first_peak
            for slot in range(blocks):
                peak = jnp.maximum(peak, jnp.max(scores(slot), axis=1, keepdims=True))
            factor = jnp.exp(first_peak - peak)
            total = first_total * factor
            summed = summed_ref[:, columns] * factor
            for slot in range(blocks):
                weight = jnp.exp(scores(slot) - peak)
                total = total + jnp.sum(weight, axis=1, keepdims=True)
                start = slot * span + (local_heads + head) * HD
                summed = summed + jnp.dot(
                    weight.astype(jnp.bfloat16),
                    source_ref[:, start : start + HD],
                    preferred_element_type=jnp.float32,
                )
            out_ref[:, columns] = (summed / total).astype(out_ref.dtype)


def attend(query, query_segment, key_segment, first, second, local_heads):
    rows = query.shape[0]
    grid = (local_heads, TOPK)
    combos = local_heads * TOPK
    scale = 1.0 / math.sqrt(HD)
    tile = pl.BlockSpec((rows, HD), lambda h, e: (0, e * local_heads + h))

    def column_spec(base):
        return pl.BlockSpec((rows, HD), lambda h, e: (0, base + h))

    def common(sources):
        specs = [
            pl.BlockSpec((rows, 1), lambda h, e: (0, 0)),
            pl.BlockSpec((len(sources), rows), lambda h, e: (0, 0)),
            tile,
        ]
        return specs

    def block_specs(sources):
        keys = [column_spec(base) for _, base in sources]
        values = [column_spec(base + local_heads) for _, base in sources]
        arrays = [array for array, _ in sources]
        return keys + values, arrays + arrays

    def cost(blocks):
        return pl.CostEstimate(
            flops=combos * 3 * blocks * 2 * rows * rows * HD,
            transcendentals=combos * blocks * rows * rows,
            bytes_accessed=query.size * 2 + blocks * rows * 2 * local_heads * HD * 2
            + 3 * combos * rows * HD * 4,
        )

    stats_shape = jax.ShapeDtypeStruct((rows, 2 * combos), jnp.float32)
    summed_shape = jax.ShapeDtypeStruct((rows, combos * HD), jnp.float32)
    stats_spec = pl.BlockSpec((rows, 2 * combos), lambda h, e: (0, 0))
    specs, arrays = block_specs(first)
    stats, summed = pl.pallas_call(
        functools.partial(first_kernel, blocks=len(first), scale=scale),
        grid=grid,
        in_specs=common(first) + specs,
        out_specs=(stats_spec, tile),
        out_shape=(stats_shape, summed_shape),
        cost_estimate=cost(len(first)),
        name="first_blocks",
    )(query_segment, key_segment[0], query, *arrays)
    source = second[0][0]
    assert all(array is source for array, _ in second)
    return pl.pallas_call(
        functools.partial(
            second_kernel, blocks=len(second), scale=scale, local_heads=local_heads
        ),
        out_shape=jax.ShapeDtypeStruct(query.shape, jnp.bfloat16),
        cost_estimate=cost(len(second)),
        name="second_blocks",
    )(query_segment, key_segment[1], query, stats, summed, source)


def body(tokens, key_weight, value_weight, queries, prompt_pages, page_table):
    block_rows = tokens.shape[0]
    width = key_weight.shape[1]
    local_heads = width // HD
    devices = lax.axis_size("seq")
    first_row = lax.axis_index("seq") * block_rows
    positions = first_row + jnp.arange(block_rows, dtype=jnp.int32)
    segment, offsets = segment_info(positions, prompt_pages)
    piece = lax.all_gather(tokens, "tp", axis=0, tiled=True)
    key_value = project(piece, key_weight, value_weight, offsets)
    direct = (1, 3, 5, 6)
    sent = {distance: from_behind(key_value, "seq", distance) for distance in direct}
    relayed = [distance for distance in range(2, BACK + 1) if distance not in direct]
    onward = from_behind(
        jnp.concatenate([sent[distance - 1] for distance in relayed], axis=1), "seq", 1
    )
    span = 2 * local_heads
    first = [(key_value, 0)] + [(sent[distance], 0) for distance in direct]
    second = [(onward, span * index) for index in range(len(relayed))]
    order = [0] + list(direct) + relayed
    key_place = positions[None, :] - block_rows * jnp.asarray(order, jnp.int32)[:, None]
    key_segment, _ = segment_info(key_place.reshape(-1), prompt_pages)
    key_segment = jnp.where(key_place >= 0, key_segment.reshape(len(order), block_rows), -1)
    key_segment = (key_segment[: len(first)], key_segment[len(first) :])
    query = queries.reshape(block_rows, TOPK * width)
    query_segment = segment[:, None]
    attended = attend(query, query_segment, key_segment, first, second, local_heads)
    attended = attended.reshape(block_rows, TOPK, width)
    pages_dev = block_rows // PAGE
    capacity = max(1, pages_dev // devices)
    owner = page_table // pages_dev
    place_on_owner = page_table % pages_dev
    page_order = jnp.arange(pages_dev, dtype=jnp.int32)
    earlier = (owner[:, None] == owner[None, :]) & (page_order[None, :] < page_order[:, None])
    rank = jnp.sum(earlier.astype(jnp.int32), axis=1)
    target = (owner[None, None, :] == jnp.arange(devices, dtype=jnp.int32)[:, None, None]) & (
        rank[None, None, :] == jnp.arange(capacity, dtype=jnp.int32)[None, :, None]
    )
    pages = key_value.reshape(pages_dev, PAGE, 2 * width)
    page_index = jnp.sum(jnp.where(target, page_order[None, None, :], 0), axis=2)
    outgoing = pages[page_index.reshape(-1)]
    labels = jnp.sum(jnp.where(target, place_on_owner[None, None, :] + 1, 0), axis=2) - 1
    incoming = lax.all_to_all(outgoing, "seq", split_axis=0, concat_axis=0, tiled=True)
    arrived = lax.all_to_all(labels, "seq", split_axis=0, concat_axis=0, tiled=True)
    slots = jnp.arange(devices * capacity, dtype=jnp.int32)
    arrived = arrived.reshape(devices * capacity, 1)
    source_slot = jnp.sum(
        jnp.where(arrived == page_order[None, :], slots[:, None], 0), axis=0
    )
    cache = incoming[source_slot].reshape(pages_dev, PAGE, 2, width)
    return (attended, cache)


def solution(mesh):
    in_specs = (P("seq", "tp"), P(None, "tp"), P(None, "tp"), P("seq", None, "tp"), P(), P("seq"))
    out_specs = (P("seq", None, "tp"), P("seq", None, None, "tp"))
    return jax.shard_map(body, mesh=mesh, in_specs=in_specs, out_specs=out_specs, check_vma=False)
```

profile of v0, /device:TPU:6, one launch (start us, length us, event | category | flops | bytes accessed | tf_op | source)
XLA Modules:
  0.0 175.5 jit_solution(464000253083755105)
XLA Ops:
  7.2 0.0 copy-start.10
  7.2 0.0 all-gather.2.cloned.1.call-start
  7.2 0.7 all-gather.2.cloned.1.call-update
  7.9 0.2 convert_reduce_fusion.1
  8.1 0.1 select_reduce_fusion.1
  8.2 0.7 copy.24
  8.9 12.6 %all-to-all-start.1 = ((s32[64,1,1]{2,1,0:T(1,128)}), s32[64,1,1]{2,1,0:T(1,128)S(1)}, u32[]{:S(2)}, u32[]{:S(2)}) async-start(s32[64,1,1]{2,1,0:T(1,128)} %copy.24), calls=%async_computation.1 | async-start | bytes 65536 | tf_op jit(solution)/shard_map/all_to_all | solution.py:279
  21.6 0.0 copy-start.7
  21.6 0.6 copy-done.7
  22.2 0.1 copy.21
  22.4 0.1 multiply_reduce_fusion
  22.5 0.1 fusion.2
  22.6 0.5 fusion
  23.1 0.8 pad_maximum_fusion.1
  24.0 24.2 %all-gather.2.cloned.1.call-done.piece_ref = bf16[2048,256]{1,0:T(8,128)(2,1)} async-done(((bf16[256,256]{1,0:T(8,128)(2,1)}), bf16[2048,256]{1,0:T(8,128)(2,1)}) %all-gather.2.cloned.1.call-update) | async-done | bytes 1048592 | tf_op jit(solution)/shard_map/all_gather | solution.py:244
  48.2 3.4 %project_rotate.1.refs_0_.refs_5_ = bf16[256,512]{1,0:T(8,128)(2,1)} custom-call(bf16[2048,256]{1,0:T(8,128)(2,1)} %all-gather.2.cloned.1.call-done.piece_ref, bf16[2048,256]{1,0:T(8,128)(2,1)} %key_weight_ref.1, bf16[2048,256]{1,0:T(8,128)(2,1)} %value_weight_ref.1, f32[256,128]{1,0:T(8,128)} %get-tuple-element.15.cosine_ref, ...), custom_call_target="tpu_custom_call" | custom-call | flops 536870912 | bytes 3407872 | tf_op jit(solution)/shard_map/project_rotate/pallas_call | solution.py:72
  51.6 2.6 %gather_fusion = bf16[64,16,512]{2,1,0:T(8,128)(2,1)} fusion(bf16[16,16,512]{2,1,0:T(8,128)(2,1)} %bitcast.16, s32[1024]{0:T(1024)S(1)} %pad_clamp_fusion.1), kind=kCustom, calls=%fused_computation | custom fusion | bytes 2097408 | tf_op jit(solution)/shard_map/gather | solution.py:276
  54.1 0.0 all-to-all-done.1
  54.1 10.6 %all-to-all-start = ((bf16[64,16,512]{2,1,0:T(8,128)(2,1)}), bf16[64,16,512]{2,1,0:T(8,128)(2,1)S(1)}, u32[]{:S(2)}, u32[]{:S(2)}) async-start(bf16[64,16,512]{2,1,0:T(8,128)(2,1)} %gather_fusion), calls=%async_computation | async-start | bytes 2097152 | tf_op jit(solution)/shard_map/all_to_all | solution.py:278
  64.8 0.1 broadcast_add_fusion
  64.8 3.4 %collective-permute-start = (bf16[256,512]{1,0:T(8,128)(2,1)S(1)}, bf16[256,512]{1,0:T(8,128)(2,1)S(1)}, u32[]{:S(2)}, u32[]{:S(2)}) collective-permute-start(bf16[256,512]{1,0:T(8,128)(2,1)S(1)} %copy-done), channel_id=1, source_target_pairs={{0,8},{8,16},{16,24},{24,32},{32,40},{40,48},{48,56},{56,64},{64,7... | collective-permute-start | bytes 786440 | tf_op jit(solution)/shard_map/ppermute | solution.py:21
  68.2 6.4 %collective-permute-start.1 = (bf16[256,512]{1,0:T(8,128)(2,1)S(1)}, bf16[256,512]{1,0:T(8,128)(2,1)S(1)}, u32[]{:S(2)}, u32[]{:S(2)}) collective-permute-start(bf16[256,512]{1,0:T(8,128)(2,1)S(1)} %copy-done), channel_id=1, source_target_pairs={{0,24},{8,32},{16,40},{24,48},{32,56},{40,64},{48,72},{56,80},{64,... | collective-permute-start | bytes 786440 | tf_op jit(solution)/shard_map/ppermute | solution.py:21
  74.6 0.1 convert_reduce_fusion
  74.7 0.8 copy.23.query_segment_ref
  75.5 0.1 compare_select_fusion.1
  75.6 0.6 slice.12.key_segment_ref
  76.2 0.7 copy.25
  76.9 1.2 reduce.3
  78.1 21.6 %collective-permute-done.refs_1_.refs_6_ = bf16[256,512]{1,0:T(8,128)(2,1)S(1)} collective-permute-done((bf16[256,512]{1,0:T(8,128)(2,1)S(1)}, bf16[256,512]{1,0:T(8,128)(2,1)S(1)}, u32[]{:S(2)}, u32[]{:S(2)}) %collective-permute-start) | collective-permute-done | bytes 262176 | tf_op jit(solution)/shard_map/ppermute | solution.py:21
  99.7 14.7 %collective-permute-done.1.refs_2_.refs_7_ = bf16[256,512]{1,0:T(8,128)(2,1)S(1)} collective-permute-done((bf16[256,512]{1,0:T(8,128)(2,1)S(1)}, bf16[256,512]{1,0:T(8,128)(2,1)S(1)}, u32[]{:S(2)}, u32[]{:S(2)}) %collective-permute-start.1) | collective-permute-done | bytes 262176 | tf_op jit(solution)/shard_map/ppermute | solution.py:21
  114.4 0.1 pad_maximum_fusion
  114.5 0.0 copy-done.3
  114.5 0.6 copy-done.4
  115.1 2.7 %collective-permute-start.4 = (bf16[256,1024]{1,0:T(8,128)(2,1)S(1)}, bf16[256,1024]{1,0:T(8,128)(2,1)S(1)}, u32[]{:S(2)}, u32[]{:S(2)}) collective-permute-start(bf16[256,1024]{1,0:T(8,128)(2,1)S(1)} %pad_maximum_fusion), channel_id=1, source_target_pairs={{0,8},{8,16},{16,24},{24,32},{32,40},{40,48},{48,56},{56,64},{64,7... | collective-permute-start | bytes 1572872 | tf_op jit(solution)/shard_map/ppermute | solution.py:21
  117.8 0.1 select_reduce_fusion
  117.9 3.0 %collective-permute-start.2 = (bf16[256,512]{1,0:T(8,128)(2,1)S(1)}, bf16[256,512]{1,0:T(8,128)(2,1)S(1)}, u32[]{:S(2)}, u32[]{:S(2)}) collective-permute-start(bf16[256,512]{1,0:T(8,128)(2,1)S(1)} %copy-done), channel_id=1, source_target_pairs={{0,40},{8,48},{16,56},{24,64},{32,72},{40,80},{48,88},{56,96},{64,... | collective-permute-start | bytes 786440 | tf_op jit(solution)/shard_map/ppermute | solution.py:21
  120.9 3.1 %collective-permute-start.3 = (bf16[256,512]{1,0:T(8,128)(2,1)S(1)}, bf16[256,512]{1,0:T(8,128)(2,1)S(1)}, u32[]{:S(2)}, u32[]{:S(2)}) collective-permute-start(bf16[256,512]{1,0:T(8,128)(2,1)S(1)} %copy-done), channel_id=1, source_target_pairs={{0,48},{8,56},{16,64},{24,72},{32,80},{40,88},{48,96},{56,104},{64... | collective-permute-start | bytes 786440 | tf_op jit(solution)/shard_map/ppermute | solution.py:21
  124.1 17.5 %collective-permute-done.2.refs_3_.refs_8_ = bf16[256,512]{1,0:T(8,128)(2,1)S(1)} collective-permute-done((bf16[256,512]{1,0:T(8,128)(2,1)S(1)}, bf16[256,512]{1,0:T(8,128)(2,1)S(1)}, u32[]{:S(2)}, u32[]{:S(2)}) %collective-permute-start.2) | collective-permute-done | bytes 262176 | tf_op jit(solution)/shard_map/ppermute | solution.py:21
  141.5 13.3 %collective-permute-done.3.refs_4_.refs_9_ = bf16[256,512]{1,0:T(8,128)(2,1)S(1)} collective-permute-done((bf16[256,512]{1,0:T(8,128)(2,1)S(1)}, bf16[256,512]{1,0:T(8,128)(2,1)S(1)}, u32[]{:S(2)}, u32[]{:S(2)}) %collective-permute-start.3) | collective-permute-done | bytes 262176 | tf_op jit(solution)/shard_map/ppermute | solution.py:21
  154.9 0.7 copy-done.9
  155.6 5.6 %first_blocks.1 = (f32[256,8]{1,0:T(8,128)}, f32[256,512]{1,0:T(8,128)}) custom-call(s32[256,1]{1,0:T(8,128)} %copy.23.query_segment_ref, s32[5,256]{1,0:T(8,128)} %bitcast.20, bf16[256,512]{1,0:T(8,128)(2,1)} %bitcast.17, bf16[256,512]{1,0:T(8,128)(2,1)} %project_rotate.1.refs_0_.refs_5_, bf16[256,512]{1,0:T(8,128)(2,1)} %copy-done.3, ...), custom_call_target="tpu_custom_call" | custom-call | flops 1006632960 | bytes 3145728 | tf_op jit(solution)/shard_map/first_blocks/pallas_call | solution.py:215
  161.2 0.0 collective-permute-done.4.source_ref
  161.2 0.8 copy-done.1
  162.0 3.6 %second_blocks.1 = bf16[256,512]{1,0:T(8,128)(2,1)} custom-call(s32[256,1]{1,0:T(8,128)} %copy.23.query_segment_ref, s32[2,256]{1,0:T(2,128)} %slice.12.key_segment_ref, bf16[256,512]{1,0:T(8,128)(2,1)} %bitcast.18, f32[256,8]{1,0:T(8,128)} %get-tuple-element.4.stats_ref, f32[256,512]{1,0:T(8,128)} %get-tuple-element.5.summed_ref, bf16[256,1024]{1,0:T(8,128)(2,1)} %copy-done.1), custom_call_target="tpu_custom_call" | custom-call | flops 402653184 | bytes 2359296 | tf_op jit(solution)/shard_map/second_blocks/pallas_call | solution.py:226
  165.6 1.7 reshape.265
  167.4 0.0 all-to-all-done
  167.4 0.6 gather_fusion.1
  167.9 0.8 reshape.267
  (28 shorter events, 0.1 us)
Async XLA Ops:
  7.2 0.7 copy-start.10
  7.2 41.0 %all-gather.2.cloned.1.call-start = ((), (), s32[]{:S(2)}) async-start(), calls=%async_computation.2 | async-start | bytes 1179648 | tf_op jit(solution)/shard_map/all_gather | solution.py:244
  8.9 45.2 %all-to-all-start.1 = ((s32[64,1,1]{2,1,0:T(1,128)}), s32[64,1,1]{2,1,0:T(1,128)S(1)}, u32[]{:S(2)}, u32[]{:S(2)}) async-start(s32[64,1,1]{2,1,0:T(1,128)} %copy.24), calls=%async_computation.1 | async-start | bytes 65536 | tf_op jit(solution)/shard_map/all_to_all | solution.py:279
  21.6 0.7 copy-start.7
  54.1 10.6 %copy-start.6 = (s32[7]{0:T(128)S(1)}, s32[7]{0:T(128)}, u32[]{:S(2)}) copy-start(s32[7]{0:T(128)} %constant.68) | copy-start | bytes 88
  54.1 10.7 %copy-start = (bf16[256,512]{1,0:T(8,128)(2,1)S(1)}, bf16[256,512]{1,0:T(8,128)(2,1)}, u32[]{:S(2)}) copy-start(bf16[256,512]{1,0:T(8,128)(2,1)} %project_rotate.1.refs_0_.refs_5_) | copy-start | bytes 786436
  54.1 22.1 %copy-start.2 = (bf16[256,2,256]{2,1,0:T(2,128)(2,1)S(1)}, bf16[256,2,256]{2,1,0:T(2,128)(2,1)}, u32[]{:S(2)}) copy-start(bf16[256,2,256]{2,1,0:T(2,128)(2,1)} %param.10) | copy-start | bytes 786436
  54.1 113.2 %all-to-all-start = ((bf16[64,16,512]{2,1,0:T(8,128)(2,1)}), bf16[64,16,512]{2,1,0:T(8,128)(2,1)S(1)}, u32[]{:S(2)}, u32[]{:S(2)}) async-start(bf16[64,16,512]{2,1,0:T(8,128)(2,1)} %gather_fusion), calls=%async_computation | async-start | bytes 2097152 | tf_op jit(solution)/shard_map/all_to_all | solution.py:278
  64.8 34.9 %collective-permute-start = (bf16[256,512]{1,0:T(8,128)(2,1)S(1)}, bf16[256,512]{1,0:T(8,128)(2,1)S(1)}, u32[]{:S(2)}, u32[]{:S(2)}) collective-permute-start(bf16[256,512]{1,0:T(8,128)(2,1)S(1)} %copy-done), channel_id=1, source_target_pairs={{0,8},{8,16},{16,24},{24,32},{32,40},{40,48},{48,56},{56,64},{64,7... | collective-permute-start | bytes 786440 | tf_op jit(solution)/shard_map/ppermute | solution.py:21
  68.2 46.2 %collective-permute-start.1 = (bf16[256,512]{1,0:T(8,128)(2,1)S(1)}, bf16[256,512]{1,0:T(8,128)(2,1)S(1)}, u32[]{:S(2)}, u32[]{:S(2)}) collective-permute-start(bf16[256,512]{1,0:T(8,128)(2,1)S(1)} %copy-done), channel_id=1, source_target_pairs={{0,24},{8,32},{16,40},{24,48},{32,56},{40,64},{48,72},{56,80},{64,... | collective-permute-start | bytes 786440 | tf_op jit(solution)/shard_map/ppermute | solution.py:21
  75.6 1.3 copy-start.5
  99.7 14.7 %copy-start.3 = (bf16[256,512]{1,0:T(8,128)(2,1)}, bf16[256,512]{1,0:T(8,128)(2,1)S(1)}, u32[]{:S(2)}) copy-start(bf16[256,512]{1,0:T(8,128)(2,1)S(1)} %collective-permute-done.refs_1_.refs_6_) | copy-start | bytes 786436
  114.4 0.7 copy-start.4
  115.1 46.1 %collective-permute-start.4 = (bf16[256,1024]{1,0:T(8,128)(2,1)S(1)}, bf16[256,1024]{1,0:T(8,128)(2,1)S(1)}, u32[]{:S(2)}, u32[]{:S(2)}) collective-permute-start(bf16[256,1024]{1,0:T(8,128)(2,1)S(1)} %pad_maximum_fusion), channel_id=1, source_target_pairs={{0,8},{8,16},{16,24},{24,32},{32,40},{40,48},{48,56},{56,64},{64,7... | collective-permute-start | bytes 1572872 | tf_op jit(solution)/shard_map/ppermute | solution.py:21
  117.9 23.6 %collective-permute-start.2 = (bf16[256,512]{1,0:T(8,128)(2,1)S(1)}, bf16[256,512]{1,0:T(8,128)(2,1)S(1)}, u32[]{:S(2)}, u32[]{:S(2)}) collective-permute-start(bf16[256,512]{1,0:T(8,128)(2,1)S(1)} %copy-done), channel_id=1, source_target_pairs={{0,40},{8,48},{16,56},{24,64},{32,72},{40,80},{48,88},{56,96},{64,... | collective-permute-start | bytes 786440 | tf_op jit(solution)/shard_map/ppermute | solution.py:21
  120.9 33.9 %collective-permute-start.3 = (bf16[256,512]{1,0:T(8,128)(2,1)S(1)}, bf16[256,512]{1,0:T(8,128)(2,1)S(1)}, u32[]{:S(2)}, u32[]{:S(2)}) collective-permute-start(bf16[256,512]{1,0:T(8,128)(2,1)S(1)} %copy-done), channel_id=1, source_target_pairs={{0,48},{8,56},{16,64},{24,72},{32,80},{40,88},{48,96},{56,104},{64... | collective-permute-start | bytes 786440 | tf_op jit(solution)/shard_map/ppermute | solution.py:21
  141.5 13.3 %copy-start.8 = (bf16[256,512]{1,0:T(8,128)(2,1)}, bf16[256,512]{1,0:T(8,128)(2,1)S(1)}, u32[]{:S(2)}) copy-start(bf16[256,512]{1,0:T(8,128)(2,1)S(1)} %collective-permute-done.2.refs_3_.refs_8_) | copy-start | bytes 786436
  154.8 0.7 copy-start.9
  161.2 0.8 copy-start.1
Sparse Core Ops, SparseCore 0:
  10.1 38.0 all-gather.1
where the time goes:
time: 176 us
  waiting for transfers between devices  92 us (52%)
  starting transfers between devices  41.8 us (24%)
  between operations  14.3 us (8%)
  Pallas kernels  12.6 us (7%)
  local copies, waits for them, and re-layouts  11.3 us (6%)
  other arithmetic  3.58 us (2%)
    ppermute x5, waiting for transfers between devices, from_behind(): return lax.ppermute(value, axis, pairs)  67 us
    all_gather x1, waiting for transfers between devices, body(): piece = lax.all_gather(tokens, 'tp', axis=0, tiled=True)  24.2 us
    ppermute x5, starting transfers between devices, from_behind(): return lax.ppermute(value, axis, pairs)  18.6 us
    all_to_all x1, starting transfers between devices, body(): lax.all_to_all(labels, 'seq', split_axis=0, concat_axis=0, tiled=True)  12.6 us
    all_to_all x1, starting transfers between devices, body(): lax.all_to_all(outgoing, 'seq', split_axis=0, concat_axis=0, tiled=True)  10.6 us
    pallas_call x1, Pallas kernels, attend(): pl.pallas_call(functools.partial(first_kernel, blocks=len(first), scale=s...  5.62 us
    pallas_call x1, Pallas kernels, attend(): pl.pallas_call(functools.partial(second_kernel, blocks=len(second), scale...  3.63 us
    unnamed x23, local copies, waits for them, and re-layouts  3.55 us
  transfers between devices with their start and end apart: 8, of which 5 were waited for; matrix products, arithmetic and copies ran while one was open for 6% of the time, Pallas kernels for 7%

commit v1 on v0

--- a/solution.py
+++ b/solution.py
@@ -173,7 +173,7 @@
                     source_ref[:, start : start + HD],
                     preferred_element_type=jnp.float32,
                 )
-            out_ref[:, columns] = (summed / total).astype(out_ref.dtype)
+            out_ref[:, expert, head * HD : (head + 1) * HD] = (summed / total).astype(out_ref.dtype)
 
 
 def attend(query, query_segment, key_segment, first, second, local_heads):
@@ -227,7 +227,7 @@
         functools.partial(
             second_kernel, blocks=len(second), scale=scale, local_heads=local_heads
         ),
-        out_shape=jax.ShapeDtypeStruct(query.shape, jnp.bfloat16),
+        out_shape=jax.ShapeDtypeStruct((rows, TOPK, combos * HD // TOPK), jnp.bfloat16),
         cost_estimate=cost(len(second)),
         name="second_blocks",
     )(query_segment, key_segment[1], query, stats, summed, source)
@@ -260,7 +260,6 @@
     query = queries.reshape(block_rows, TOPK * width)
     query_segment = segment[:, None]
     attended = attend(query, query_segment, key_segment, first, second, local_heads)
-    attended = attended.reshape(block_rows, TOPK, width)
     pages_dev = block_rows // PAGE
     capacity = max(1, pages_dev // devices)
     owner = page_table // pages_dev

time: 176 us -> 175 us (level)
  transfers between devices with their start and end apart: 8 -> 8, of which waited for: 5 -> 5; matrix products, arithmetic and copies ran while one was open for 6% -> 5% of each run, Pallas kernels for 7% -> 7%
where the time goes in v1:
time: 175 us; the launch traced here: 174 us
  waiting for transfers between devices  92 us (53%)
  starting transfers between devices  41.8 us (24%)
  between operations  14.3 us (8%)
  Pallas kernels  13.1 us (7%)
  local copies, waits for them, and re-layouts  9.59 us (5%)
  other arithmetic  3.58 us (2%)
    ppermute x5, waiting for transfers between devices, from_behind(): return lax.ppermute(value, axis, pairs)  67 us
    all_gather x1, waiting for transfers between devices, body(): piece = lax.all_gather(tokens, 'tp', axis=0, tiled=True)  24.2 us
    ppermute x5, starting transfers between devices, from_behind(): return lax.ppermute(value, axis, pairs)  18.6 us
    all_to_all x1, starting transfers between devices, body(): lax.all_to_all(labels, 'seq', split_axis=0, concat_axis=0, tiled=True)  12.6 us
    all_to_all x1, starting transfers between devices, body(): lax.all_to_all(outgoing, 'seq', split_axis=0, concat_axis=0, tiled=True)  10.6 us
    pallas_call x1, Pallas kernels, attend(): pl.pallas_call(functools.partial(first_kernel, blocks=len(first), scale=s...  5.62 us
    pallas_call x1, Pallas kernels, attend(): pl.pallas_call(functools.partial(second_kernel, blocks=len(second), scale...  4.07 us
    unnamed x23, local copies, waits for them, and re-layouts  3.55 us
  transfers between devices with their start and end apart: 8, of which 5 were waited for; matrix products, arithmetic and copies ran while one was open for 5% of the time, Pallas kernels for 7%

profile of v1, /device:TPU:6, one launch (start us, length us, event | category | flops | bytes accessed | tf_op | source)
XLA Modules:
  0.0 174.3 jit_solution(7578750352450583409)
XLA Ops:
  7.2 0.0 copy-start.10
  7.2 0.0 all-gather.2.cloned.1.call-start
  7.2 0.7 all-gather.2.cloned.1.call-update
  7.9 0.0 copy-done.10
  7.9 0.2 convert_reduce_fusion.1
  8.1 0.1 select_reduce_fusion.1
  8.2 0.7 copy.24
  8.9 12.6 %all-to-all-start.1 = ((s32[64,1,1]{2,1,0:T(1,128)}), s32[64,1,1]{2,1,0:T(1,128)S(1)}, u32[]{:S(2)}, u32[]{:S(2)}) async-start(s32[64,1,1]{2,1,0:T(1,128)} %copy.24), calls=%async_computation.1 | async-start | bytes 65536 | tf_op jit(solution)/shard_map/all_to_all | solution.py:278
  21.6 0.0 copy-start.7
  21.6 0.6 copy-done.7
  22.2 0.1 copy.21
  22.4 0.1 multiply_reduce_fusion
  22.5 0.1 fusion.2
  22.6 0.5 fusion
  23.1 0.8 pad_maximum_fusion.1
  24.0 24.2 %all-gather.2.cloned.1.call-done.piece_ref = bf16[2048,256]{1,0:T(8,128)(2,1)} async-done(((bf16[256,256]{1,0:T(8,128)(2,1)}), bf16[2048,256]{1,0:T(8,128)(2,1)}) %all-gather.2.cloned.1.call-update) | async-done | bytes 1048592 | tf_op jit(solution)/shard_map/all_gather | solution.py:244
  48.2 3.4 %project_rotate.1.refs_0_.refs_5_ = bf16[256,512]{1,0:T(8,128)(2,1)} custom-call(bf16[2048,256]{1,0:T(8,128)(2,1)} %all-gather.2.cloned.1.call-done.piece_ref, bf16[2048,256]{1,0:T(8,128)(2,1)} %key_weight_ref.1, bf16[2048,256]{1,0:T(8,128)(2,1)} %value_weight_ref.1, f32[256,128]{1,0:T(8,128)} %get-tuple-element.15.cosine_ref, ...), custom_call_target="tpu_custom_call" | custom-call | flops 536870912 | bytes 3407872 | tf_op jit(solution)/shard_map/project_rotate/pallas_call | solution.py:72
  51.6 2.6 %gather_fusion = bf16[64,16,512]{2,1,0:T(8,128)(2,1)} fusion(bf16[16,16,512]{2,1,0:T(8,128)(2,1)} %bitcast.16, s32[1024]{0:T(1024)S(1)} %pad_clamp_fusion.1), kind=kCustom, calls=%fused_computation | custom fusion | bytes 2097408 | tf_op jit(solution)/shard_map/gather | solution.py:275
  54.1 0.0 all-to-all-done.1
  54.1 10.6 %all-to-all-start = ((bf16[64,16,512]{2,1,0:T(8,128)(2,1)}), bf16[64,16,512]{2,1,0:T(8,128)(2,1)S(1)}, u32[]{:S(2)}, u32[]{:S(2)}) async-start(bf16[64,16,512]{2,1,0:T(8,128)(2,1)} %gather_fusion), calls=%async_computation | async-start | bytes 2097152 | tf_op jit(solution)/shard_map/all_to_all | solution.py:277
  64.8 0.1 broadcast_add_fusion
  64.8 3.4 %collective-permute-start = (bf16[256,512]{1,0:T(8,128)(2,1)S(1)}, bf16[256,512]{1,0:T(8,128)(2,1)S(1)}, u32[]{:S(2)}, u32[]{:S(2)}) collective-permute-start(bf16[256,512]{1,0:T(8,128)(2,1)S(1)} %copy-done), channel_id=1, source_target_pairs={{0,8},{8,16},{16,24},{24,32},{32,40},{40,48},{48,56},{56,64},{64,7... | collective-permute-start | bytes 786440 | tf_op jit(solution)/shard_map/ppermute | solution.py:21
  68.2 6.4 %collective-permute-start.1 = (bf16[256,512]{1,0:T(8,128)(2,1)S(1)}, bf16[256,512]{1,0:T(8,128)(2,1)S(1)}, u32[]{:S(2)}, u32[]{:S(2)}) collective-permute-start(bf16[256,512]{1,0:T(8,128)(2,1)S(1)} %copy-done), channel_id=1, source_target_pairs={{0,24},{8,32},{16,40},{24,48},{32,56},{40,64},{48,72},{56,80},{64,... | collective-permute-start | bytes 786440 | tf_op jit(solution)/shard_map/ppermute | solution.py:21
  74.6 0.1 convert_reduce_fusion
  74.7 0.8 copy.23.query_segment_ref
  75.5 0.1 compare_select_fusion.1
  75.6 0.6 slice.12.key_segment_ref
  76.2 0.7 copy.25
  76.9 1.2 reduce.3
  78.1 21.6 %collective-permute-done.refs_1_.refs_6_ = bf16[256,512]{1,0:T(8,128)(2,1)S(1)} collective-permute-done((bf16[256,512]{1,0:T(8,128)(2,1)S(1)}, bf16[256,512]{1,0:T(8,128)(2,1)S(1)}, u32[]{:S(2)}, u32[]{:S(2)}) %collective-permute-start) | collective-permute-done | bytes 262176 | tf_op jit(solution)/shard_map/ppermute | solution.py:21
  99.7 14.7 %collective-permute-done.1.refs_2_.refs_7_ = bf16[256,512]{1,0:T(8,128)(2,1)S(1)} collective-permute-done((bf16[256,512]{1,0:T(8,128)(2,1)S(1)}, bf16[256,512]{1,0:T(8,128)(2,1)S(1)}, u32[]{:S(2)}, u32[]{:S(2)}) %collective-permute-start.1) | collective-permute-done | bytes 262176 | tf_op jit(solution)/shard_map/ppermute | solution.py:21
  114.4 0.1 pad_maximum_fusion
  114.5 0.0 copy-done.3
  114.5 0.6 copy-done.4
  115.1 2.7 %collective-permute-start.4 = (bf16[256,1024]{1,0:T(8,128)(2,1)S(1)}, bf16[256,1024]{1,0:T(8,128)(2,1)S(1)}, u32[]{:S(2)}, u32[]{:S(2)}) collective-permute-start(bf16[256,1024]{1,0:T(8,128)(2,1)S(1)} %pad_maximum_fusion), channel_id=1, source_target_pairs={{0,8},{8,16},{16,24},{24,32},{32,40},{40,48},{48,56},{56,64},{64,7... | collective-permute-start | bytes 1572872 | tf_op jit(solution)/shard_map/ppermute | solution.py:21
  117.8 0.1 select_reduce_fusion
  117.9 3.0 %collective-permute-start.2 = (bf16[256,512]{1,0:T(8,128)(2,1)S(1)}, bf16[256,512]{1,0:T(8,128)(2,1)S(1)}, u32[]{:S(2)}, u32[]{:S(2)}) collective-permute-start(bf16[256,512]{1,0:T(8,128)(2,1)S(1)} %copy-done), channel_id=1, source_target_pairs={{0,40},{8,48},{16,56},{24,64},{32,72},{40,80},{48,88},{56,96},{64,... | collective-permute-start | bytes 786440 | tf_op jit(solution)/shard_map/ppermute | solution.py:21
  120.9 3.1 %collective-permute-start.3 = (bf16[256,512]{1,0:T(8,128)(2,1)S(1)}, bf16[256,512]{1,0:T(8,128)(2,1)S(1)}, u32[]{:S(2)}, u32[]{:S(2)}) collective-permute-start(bf16[256,512]{1,0:T(8,128)(2,1)S(1)} %copy-done), channel_id=1, source_target_pairs={{0,48},{8,56},{16,64},{24,72},{32,80},{40,88},{48,96},{56,104},{64... | collective-permute-start | bytes 786440 | tf_op jit(solution)/shard_map/ppermute | solution.py:21
  124.1 17.5 %collective-permute-done.2.refs_3_.refs_8_ = bf16[256,512]{1,0:T(8,128)(2,1)S(1)} collective-permute-done((bf16[256,512]{1,0:T(8,128)(2,1)S(1)}, bf16[256,512]{1,0:T(8,128)(2,1)S(1)}, u32[]{:S(2)}, u32[]{:S(2)}) %collective-permute-start.2) | collective-permute-done | bytes 262176 | tf_op jit(solution)/shard_map/ppermute | solution.py:21
  141.5 13.3 %collective-permute-done.3.refs_4_.refs_9_ = bf16[256,512]{1,0:T(8,128)(2,1)S(1)} collective-permute-done((bf16[256,512]{1,0:T(8,128)(2,1)S(1)}, bf16[256,512]{1,0:T(8,128)(2,1)S(1)}, u32[]{:S(2)}, u32[]{:S(2)}) %collective-permute-start.3) | collective-permute-done | bytes 262176 | tf_op jit(solution)/shard_map/ppermute | solution.py:21
  154.9 0.7 copy-done.9
  155.6 5.6 %first_blocks.1 = (f32[256,8]{1,0:T(8,128)}, f32[256,512]{1,0:T(8,128)}) custom-call(s32[256,1]{1,0:T(8,128)} %copy.23.query_segment_ref, s32[5,256]{1,0:T(8,128)} %bitcast.20, bf16[256,512]{1,0:T(8,128)(2,1)} %bitcast.17, bf16[256,512]{1,0:T(8,128)(2,1)} %project_rotate.1.refs_0_.refs_5_, bf16[256,512]{1,0:T(8,128)(2,1)} %copy-done.3, ...), custom_call_target="tpu_custom_call" | custom-call | flops 1006632960 | bytes 3145728 | tf_op jit(solution)/shard_map/first_blocks/pallas_call | solution.py:215
  161.2 0.0 collective-permute-done.4.source_ref
  161.2 0.8 copy-done.1
  162.0 4.1 %second_blocks.1 = bf16[256,2,256]{2,1,0:T(2,128)(2,1)} custom-call(s32[256,1]{1,0:T(8,128)} %copy.23.query_segment_ref, s32[2,256]{1,0:T(2,128)} %slice.12.key_segment_ref, bf16[256,512]{1,0:T(8,128)(2,1)} %bitcast.18, f32[256,8]{1,0:T(8,128)} %get-tuple-element.4.stats_ref, f32[256,512]{1,0:T(8,128)} %get-tuple-element.5.summed_ref, ...), custom_call_target="tpu_custom_call" | custom-call | flops 402653184 | bytes 2359296 | tf_op jit(solution)/shard_map/second_blocks/pallas_call | solution.py:226
  166.1 0.0 all-to-all-done
  166.1 0.6 gather_fusion.1
  166.6 0.8 reshape.263
  (27 shorter events, 0.1 us)
Async XLA Ops:
  7.2 0.7 copy-start.10
  7.2 41.0 %all-gather.2.cloned.1.call-start = ((), (), s32[]{:S(2)}) async-start(), calls=%async_computation.2 | async-start | bytes 1179648 | tf_op jit(solution)/shard_map/all_gather | solution.py:244
  8.9 45.2 %all-to-all-start.1 = ((s32[64,1,1]{2,1,0:T(1,128)}), s32[64,1,1]{2,1,0:T(1,128)S(1)}, u32[]{:S(2)}, u32[]{:S(2)}) async-start(s32[64,1,1]{2,1,0:T(1,128)} %copy.24), calls=%async_computation.1 | async-start | bytes 65536 | tf_op jit(solution)/shard_map/all_to_all | solution.py:278
  21.6 0.7 copy-start.7
  54.1 10.6 %copy-start.6 = (s32[7]{0:T(128)S(1)}, s32[7]{0:T(128)}, u32[]{:S(2)}) copy-start(s32[7]{0:T(128)} %constant.68) | copy-start | bytes 88
  54.1 10.7 %copy-start = (bf16[256,512]{1,0:T(8,128)(2,1)S(1)}, bf16[256,512]{1,0:T(8,128)(2,1)}, u32[]{:S(2)}) copy-start(bf16[256,512]{1,0:T(8,128)(2,1)} %project_rotate.1.refs_0_.refs_5_) | copy-start | bytes 786436
  54.1 22.1 %copy-start.2 = (bf16[256,2,256]{2,1,0:T(2,128)(2,1)S(1)}, bf16[256,2,256]{2,1,0:T(2,128)(2,1)}, u32[]{:S(2)}) copy-start(bf16[256,2,256]{2,1,0:T(2,128)(2,1)} %param.10) | copy-start | bytes 786436
  54.1 111.9 %all-to-all-start = ((bf16[64,16,512]{2,1,0:T(8,128)(2,1)}), bf16[64,16,512]{2,1,0:T(8,128)(2,1)S(1)}, u32[]{:S(2)}, u32[]{:S(2)}) async-start(bf16[64,16,512]{2,1,0:T(8,128)(2,1)} %gather_fusion), calls=%async_computation | async-start | bytes 2097152 | tf_op jit(solution)/shard_map/all_to_all | solution.py:277
  64.8 34.9 %collective-permute-start = (bf16[256,512]{1,0:T(8,128)(2,1)S(1)}, bf16[256,512]{1,0:T(8,128)(2,1)S(1)}, u32[]{:S(2)}, u32[]{:S(2)}) collective-permute-start(bf16[256,512]{1,0:T(8,128)(2,1)S(1)} %copy-done), channel_id=1, source_target_pairs={{0,8},{8,16},{16,24},{24,32},{32,40},{40,48},{48,56},{56,64},{64,7... | collective-permute-start | bytes 786440 | tf_op jit(solution)/shard_map/ppermute | solution.py:21
  68.2 46.2 %collective-permute-start.1 = (bf16[256,512]{1,0:T(8,128)(2,1)S(1)}, bf16[256,512]{1,0:T(8,128)(2,1)S(1)}, u32[]{:S(2)}, u32[]{:S(2)}) collective-permute-start(bf16[256,512]{1,0:T(8,128)(2,1)S(1)} %copy-done), channel_id=1, source_target_pairs={{0,24},{8,32},{16,40},{24,48},{32,56},{40,64},{48,72},{56,80},{64,... | collective-permute-start | bytes 786440 | tf_op jit(solution)/shard_map/ppermute | solution.py:21
  75.6 1.3 copy-start.5
  99.7 14.7 %copy-start.3 = (bf16[256,512]{1,0:T(8,128)(2,1)}, bf16[256,512]{1,0:T(8,128)(2,1)S(1)}, u32[]{:S(2)}) copy-start(bf16[256,512]{1,0:T(8,128)(2,1)S(1)} %collective-permute-done.refs_1_.refs_6_) | copy-start | bytes 786436
  114.4 0.7 copy-start.4
  115.1 46.1 %collective-permute-start.4 = (bf16[256,1024]{1,0:T(8,128)(2,1)S(1)}, bf16[256,1024]{1,0:T(8,128)(2,1)S(1)}, u32[]{:S(2)}, u32[]{:S(2)}) collective-permute-start(bf16[256,1024]{1,0:T(8,128)(2,1)S(1)} %pad_maximum_fusion), channel_id=1, source_target_pairs={{0,8},{8,16},{16,24},{24,32},{32,40},{40,48},{48,56},{56,64},{64,7... | collective-permute-start | bytes 1572872 | tf_op jit(solution)/shard_map/ppermute | solution.py:21
  117.9 23.6 %collective-permute-start.2 = (bf16[256,512]{1,0:T(8,128)(2,1)S(1)}, bf16[256,512]{1,0:T(8,128)(2,1)S(1)}, u32[]{:S(2)}, u32[]{:S(2)}) collective-permute-start(bf16[256,512]{1,0:T(8,128)(2,1)S(1)} %copy-done), channel_id=1, source_target_pairs={{0,40},{8,48},{16,56},{24,64},{32,72},{40,80},{48,88},{56,96},{64,... | collective-permute-start | bytes 786440 | tf_op jit(solution)/shard_map/ppermute | solution.py:21
  120.9 33.9 %collective-permute-start.3 = (bf16[256,512]{1,0:T(8,128)(2,1)S(1)}, bf16[256,512]{1,0:T(8,128)(2,1)S(1)}, u32[]{:S(2)}, u32[]{:S(2)}) collective-permute-start(bf16[256,512]{1,0:T(8,128)(2,1)S(1)} %copy-done), channel_id=1, source_target_pairs={{0,48},{8,56},{16,64},{24,72},{32,80},{40,88},{48,96},{56,104},{64... | collective-permute-start | bytes 786440 | tf_op jit(solution)/shard_map/ppermute | solution.py:21
  141.5 13.3 %copy-start.8 = (bf16[256,512]{1,0:T(8,128)(2,1)}, bf16[256,512]{1,0:T(8,128)(2,1)S(1)}, u32[]{:S(2)}) copy-start(bf16[256,512]{1,0:T(8,128)(2,1)S(1)} %collective-permute-done.2.refs_3_.refs_8_) | copy-start | bytes 786436
  154.8 0.7 copy-start.9
  161.2 0.8 copy-start.1
Sparse Core Ops, SparseCore 0:
  10.1 38.0 all-gather.1
